TPU v7x, 256 devices: a whole 4x4x8 slice. The times are simulated.
256 devices in a mesh: blk: 8 (over y, x_hi), grp: 32 (over x_lo, z, core).
Axes of the slice: x: 4 (x_hi: 2, x_lo: 2; x = x_hi * 2 + x_lo), y: 4, z: 8, core: 2. Of those that a mesh axis runs over, the one named last changes fastest.
Arguments:
- position: float32 [3, 65536], P(None, ('blk', 'grp'))
- velocity: float32 [3, 65536], P(None, ('blk', 'grp')), may hold values from -3 to 3
- accel_old: float32 [3, 65536], P(None, ('blk', 'grp')), may hold values from -5 to 5
- jerk_old: float32 [3, 65536], P(None, ('blk', 'grp')), may hold values from -5 to 5
- elapsed: float32 [65536], P(('blk', 'grp')), may hold values from 0.01 to 0.1
- masses: float32 [65536], P(('blk', 'grp'))
- active_stars: int32 [8192], P(('blk', 'grp')), may hold values from 0 to 255, as said below
- neighbour_list: int32 [256, 64], P(('blk', 'grp')), may hold values from 0 to 63, as said below
- neighbour_count: int32 [256], P(('blk', 'grp')), may hold values from 1 to 64, as said below
Outputs:
- regular: float32 [6, 8192], P(None, ('blk', 'grp'))
- irregular: float32 [6, 8192], P(None, ('blk', 'grp'))
- correction: float32 [6, 8192], P(None, ('blk', 'grp'))
Inputs may be any that keep to these rules, and one draw needn't show every extreme that they name: `active_stars`: the 32 entries of one device are distinct local indices of that device's stars, all inside one block of 128 of them. `neighbour_list`: row r lists neighbour blocks for the active stars of device r, numbered within r's group (2 blocks a device, devices in grp order). Its first neighbour_count[r] entries are distinct and ascending, at most 2 of them from one device, and include the block that holds r's active stars; later entries mean nothing. `neighbour_count`: in every group along blk some device lists 2 blocks of every device of its group.
All inputs are finite; a program needn't handle non-finite values.
Results may differ from a plain program's by a relative error of at most 0.0003.
Values sent between devices are 32-bit elements; how exact they have to be, the bound alone decides.
No kernel may reach another device: no remote copies, remote signals or barrier semaphores. Data moves between devices by JAX's collectives and lax.ppermute only.
A program may use at most 64 MiB of HBM per device.

v0:
```python
import jax
import jax.numpy as jnp
from jax import lax
from jax.sharding import PartitionSpec as P

BLOCK = 128
soften_sq = 0.0001


def pair_sums(targets, sources, weight):
    gap_x = sources[0][None, :] - targets[0][:, None]
    gap_y = sources[1][None, :] - targets[1][:, None]
    gap_z = sources[2][None, :] - targets[2][:, None]
    rel_x = sources[3][None, :] - targets[3][:, None]
    rel_y = sources[4][None, :] - targets[4][:, None]
    rel_z = sources[5][None, :] - targets[5][:, None]
    dist_sq = gap_x * gap_x + gap_y * gap_y + gap_z * gap_z + soften_sq
    inverse = lax.rsqrt(dist_sq)
    scaled = weight * (inverse * inverse * inverse)
    radial = 3.0 * (gap_x * rel_x + gap_y * rel_y + gap_z * rel_z) / dist_sq
    term_list = [
        gap_x,
        gap_y,
        gap_z,
        rel_x - radial * gap_x,
        rel_y - radial * gap_y,
        rel_z - radial * gap_z,
    ]
    return jnp.stack([jnp.sum(scaled * term, axis=1) for term in term_list])


def per_device(
    position,
    velocity,
    accel_old,
    jerk_old,
    elapsed,
    masses,
    active_stars,
    neighbour_list,
    neighbour_count,
):
    moved_pos = position + elapsed * (
        velocity + elapsed * (0.5 * accel_old + elapsed * jerk_old / 6.0)
    )
    turned = velocity + elapsed * (accel_old + 0.5 * elapsed * jerk_old)
    sources = jnp.concatenate([moved_pos, turned], axis=0)
    own_set = jnp.take(sources, active_stars, axis=1)
    act_dev = active_stars.shape[0]
    block_data = jnp.concatenate([sources, masses[None, :]], axis=0)
    group = lax.all_gather(block_data, "grp", axis=1, tiled=True)
    group_src = group[:6]
    group_mass = group[6]
    targets = lax.all_gather(own_set, "blk", axis=1, tiled=True)
    blk_size = lax.axis_size("blk")
    blk_here = lax.axis_index("blk")
    block_total = group_src.shape[1] // BLOCK
    slot_total = neighbour_list.shape[1]
    own_live = jnp.arange(slot_total) < neighbour_count[0]
    near = jnp.any(
        own_live[:, None] & (neighbour_list[0][:, None] == jnp.arange(block_total)[None, :]), axis=0
    ).astype(jnp.float32)
    owner_rows = jnp.arange(blk_size)
    keep = jnp.where((owner_rows == blk_here)[:, None], 1.0 - near[None, :], 1.0)
    target_pieces = targets.reshape(6, blk_size, act_dev).transpose(1, 0, 2)

    def one_piece(items):
        target_piece, keep_piece = items
        weight = jnp.repeat(keep_piece, BLOCK)[None, :] * group_mass[None, :]
        return pair_sums(target_piece, group_src, weight)

    sums = lax.map(one_piece, (target_pieces, keep))
    partial_terms = sums.transpose(1, 0, 2).reshape(6, blk_size * act_dev)
    regular = lax.psum_scatter(partial_terms, "blk", scatter_dimension=1, tiled=True)
    near_mass = (jnp.repeat(near, BLOCK) * group_mass)[None, :]
    irregular = pair_sums(own_set, group_src, near_mass)
    accel_now = regular[:3] + irregular[:3]
    jerk_now = regular[3:] + irregular[3:]
    step_time = jnp.take(elapsed, active_stars)
    start_accel = jnp.take(accel_old, active_stars, axis=1)
    start_jerk = jnp.take(jerk_old, active_stars, axis=1)
    change = start_accel - accel_now
    snap_term = -6.0 * change - step_time * (4.0 * start_jerk + 2.0 * jerk_now)
    crackle_term = 12.0 * change + 6.0 * step_time * (start_jerk + jerk_now)
    return (regular, irregular, jnp.concatenate([snap_term, crackle_term], axis=0))


def solution(mesh):
    in_specs = (
        P(None, ("blk", "grp")),
        P(None, ("blk", "grp")),
        P(None, ("blk", "grp")),
        P(None, ("blk", "grp")),
        P(("blk", "grp")),
        P(("blk", "grp")),
        P(("blk", "grp")),
        P(("blk", "grp"), None),
        P(("blk", "grp")),
    )
    out_specs = (P(None, ("blk", "grp")), P(None, ("blk", "grp")), P(None, ("blk", "grp")))
    return jax.shard_map(
        per_device, mesh=mesh, in_specs=in_specs, out_specs=out_specs, check_vma=False
    )
```

profile of v0, /device:TPU:32, one launch (start us, length us, event | category | flops | bytes accessed | tf_op | source)
XLA Modules:
  0.0 184.2 jit_solution(8976956344711509726)
XLA Ops:
  7.9 0.8 fusion.42
  8.7 0.7 copy-done
  10.1 0.7 gather_fusion.1
  10.8 0.6 gather_fusion
  11.4 0.7 copy-done.6
  12.1 34.8 %all_gather.6 = f32[7,8192]{1,0:T(8,128)S(1)} all-gather(f32[7,256]{1,0:T(8,128)S(1)} %pad_maximum_fusion), channel_id=1, replica_groups=mesh['blk'=8,'grp'=32] {'grp'}, dimensions={1}, use_global_device_ids=true | all-gather | bytes 236544 | tf_op jit(solution)/shard_map/all_gather | solution.py:51
  47.1 34.6 %all-gather = f32[8,32,6]{1,2,0:T(8,128)S(1)} all-gather(f32[1,32,6]{1,2,0:T(8,128)S(1)} %copy.109), channel_id=1, replica_groups=mesh['blk'=8,'grp'=32] {'blk'}, dimensions={0}, use_global_device_ids=true | all-gather | bytes 6912 | tf_op jit(solution)/shard_map/all_gather | solution.py:54
  82.2 18.5 %while.10 = (s32[]{:T(128)}, f32[8,6,32]{2,1,0:T(8,128)S(1)}, f32[8,64]{1,0:T(8,128)S(1)}, f32[1,8192]{1,0:T(1,128)S(1)}, f32[6,8192]{1,0:T(8,128)S(1)}, /*index...) while((s32[]{:T(128)}, f32[8,6,32]{2,1,0:T(8,128)S(1)}, ...), condition=%wide.region_8.9_spmd, body=%wide.region_1.8_spmd.sunk | while | flops 10493767 | bytes 701913 | solution.py:72
  82.5 2.0 %fusion.58 = (f32[32]{0:T(128)S(1)}, f32[32]{0:T(128)S(1)}, f32[32]{0:T(128)S(1)}, f32[32]{0:T(128)S(1)}, f32[32]{0:T(128)S(1)}, /*index=5*/f32[32]{0:T(128)S(1)}) fusion(f32[32]{0:T(128)S(1)} %get-tuple-element.206, f32[8192]{0:T(1024)S(1)} %bitcast.131, f32[32]{0:T(128)S(1)} %get-tuple-element.208, f32[8192]{0:T(1024)S(1)} %bitcast.133, ...), kind=kLoop, calls=%fused_computation.25.clone.1 | loop fusion | flops 10485568 | bytes 230912 | tf_op jit(solution)/shard_map/while/body/eval_jaxpr/reduce_sum | solution.py:29
  84.8 2.0 %fusion.58 = (f32[32]{0:T(128)S(1)}, f32[32]{0:T(128)S(1)}, f32[32]{0:T(128)S(1)}, f32[32]{0:T(128)S(1)}, f32[32]{0:T(128)S(1)}, /*index=5*/f32[32]{0:T(128)S(1)}) fusion(f32[32]{0:T(128)S(1)} %get-tuple-element.206, f32[8192]{0:T(1024)S(1)} %bitcast.131, f32[32]{0:T(128)S(1)} %get-tuple-element.208, f32[8192]{0:T(1024)S(1)} %bitcast.133, ...), kind=kLoop, calls=%fused_computation.25.clone.1 | loop fusion | flops 10485568 | bytes 230912 | tf_op jit(solution)/shard_map/while/body/eval_jaxpr/reduce_sum | solution.py:29
  87.1 2.0 %fusion.58 = (f32[32]{0:T(128)S(1)}, f32[32]{0:T(128)S(1)}, f32[32]{0:T(128)S(1)}, f32[32]{0:T(128)S(1)}, f32[32]{0:T(128)S(1)}, /*index=5*/f32[32]{0:T(128)S(1)}) fusion(f32[32]{0:T(128)S(1)} %get-tuple-element.206, f32[8192]{0:T(1024)S(1)} %bitcast.131, f32[32]{0:T(128)S(1)} %get-tuple-element.208, f32[8192]{0:T(1024)S(1)} %bitcast.133, ...), kind=kLoop, calls=%fused_computation.25.clone.1 | loop fusion | flops 10485568 | bytes 230912 | tf_op jit(solution)/shard_map/while/body/eval_jaxpr/reduce_sum | solution.py:29
  89.4 2.0 %fusion.58 = (f32[32]{0:T(128)S(1)}, f32[32]{0:T(128)S(1)}, f32[32]{0:T(128)S(1)}, f32[32]{0:T(128)S(1)}, f32[32]{0:T(128)S(1)}, /*index=5*/f32[32]{0:T(128)S(1)}) fusion(f32[32]{0:T(128)S(1)} %get-tuple-element.206, f32[8192]{0:T(1024)S(1)} %bitcast.131, f32[32]{0:T(128)S(1)} %get-tuple-element.208, f32[8192]{0:T(1024)S(1)} %bitcast.133, ...), kind=kLoop, calls=%fused_computation.25.clone.1 | loop fusion | flops 10485568 | bytes 230912 | tf_op jit(solution)/shard_map/while/body/eval_jaxpr/reduce_sum | solution.py:29
  91.8 2.0 %fusion.58 = (f32[32]{0:T(128)S(1)}, f32[32]{0:T(128)S(1)}, f32[32]{0:T(128)S(1)}, f32[32]{0:T(128)S(1)}, f32[32]{0:T(128)S(1)}, /*index=5*/f32[32]{0:T(128)S(1)}) fusion(f32[32]{0:T(128)S(1)} %get-tuple-element.206, f32[8192]{0:T(1024)S(1)} %bitcast.131, f32[32]{0:T(128)S(1)} %get-tuple-element.208, f32[8192]{0:T(1024)S(1)} %bitcast.133, ...), kind=kLoop, calls=%fused_computation.25.clone.1 | loop fusion | flops 10485568 | bytes 230912 | tf_op jit(solution)/shard_map/while/body/eval_jaxpr/reduce_sum | solution.py:29
  94.1 2.0 %fusion.58 = (f32[32]{0:T(128)S(1)}, f32[32]{0:T(128)S(1)}, f32[32]{0:T(128)S(1)}, f32[32]{0:T(128)S(1)}, f32[32]{0:T(128)S(1)}, /*index=5*/f32[32]{0:T(128)S(1)}) fusion(f32[32]{0:T(128)S(1)} %get-tuple-element.206, f32[8192]{0:T(1024)S(1)} %bitcast.131, f32[32]{0:T(128)S(1)} %get-tuple-element.208, f32[8192]{0:T(1024)S(1)} %bitcast.133, ...), kind=kLoop, calls=%fused_computation.25.clone.1 | loop fusion | flops 10485568 | bytes 230912 | tf_op jit(solution)/shard_map/while/body/eval_jaxpr/reduce_sum | solution.py:29
  96.4 2.0 %fusion.58 = (f32[32]{0:T(128)S(1)}, f32[32]{0:T(128)S(1)}, f32[32]{0:T(128)S(1)}, f32[32]{0:T(128)S(1)}, f32[32]{0:T(128)S(1)}, /*index=5*/f32[32]{0:T(128)S(1)}) fusion(f32[32]{0:T(128)S(1)} %get-tuple-element.206, f32[8192]{0:T(1024)S(1)} %bitcast.131, f32[32]{0:T(128)S(1)} %get-tuple-element.208, f32[8192]{0:T(1024)S(1)} %bitcast.133, ...), kind=kLoop, calls=%fused_computation.25.clone.1 | loop fusion | flops 10485568 | bytes 230912 | tf_op jit(solution)/shard_map/while/body/eval_jaxpr/reduce_sum | solution.py:29
  98.7 2.0 %fusion.58 = (f32[32]{0:T(128)S(1)}, f32[32]{0:T(128)S(1)}, f32[32]{0:T(128)S(1)}, f32[32]{0:T(128)S(1)}, f32[32]{0:T(128)S(1)}, /*index=5*/f32[32]{0:T(128)S(1)}) fusion(f32[32]{0:T(128)S(1)} %get-tuple-element.206, f32[8192]{0:T(1024)S(1)} %bitcast.131, f32[32]{0:T(128)S(1)} %get-tuple-element.208, f32[8192]{0:T(1024)S(1)} %bitcast.133, ...), kind=kLoop, calls=%fused_computation.25.clone.1 | loop fusion | flops 10485568 | bytes 230912 | tf_op jit(solution)/shard_map/while/body/eval_jaxpr/reduce_sum | solution.py:29
  100.8 0.8 copy.119
  101.8 2.0 %fusion.29 = (f32[32]{0:T(128)S(1)}, f32[32]{0:T(128)S(1)}, f32[32]{0:T(128)S(1)}, f32[32]{0:T(128)S(1)}, f32[32]{0:T(128)S(1)}, /*index=5*/f32[32]{0:T(128)S(1)}) fusion(f32[32]{0:T(128)S(1)} %get-tuple-element.111, f32[8192]{0:T(1024)S(1)} %bitcast.141, f32[32]{0:T(128)S(1)} %get-tuple-element.108, f32[8192]{0:T(1024)S(1)} %bitcast.143, ...), kind=kLoop, calls=%fused_computation.74 | loop fusion | flops 10485568 | bytes 230912 | tf_op jit(solution)/shard_map/reduce_sum | solution.py:29
  104.1 0.6 gather_fusion.2
  104.8 0.6 gather_fusion.3
  105.4 0.6 stack.52
  106.0 69.3 %reduce-scatter.4.cloned.1.call-done = f32[32,6]{1,0:T(8,128)} async-done(((f32[256,6]{1,0:T(8,128)}), f32[32,6]{1,0:T(8,128)}) %reduce-scatter.4.cloned.1.call-update) | async-done | bytes 784
  175.3 0.8 copy.118
  176.7 0.6 pad_maximum_fusion.2
  (92 shorter events, 4.9 us)
Async XLA Ops:
  7.2 168.2 %reduce-scatter.4.cloned.1.call-start = ((), (), s32[]{:S(2)}) async-start(), calls=%async_computation.1 | async-start | bytes 147456
  7.2 2.2 %copy-start.5 = (f32[3,256]{1,0:T(4,128)S(1)}, f32[3,256]{1,0:T(4,128)}, u32[]{:S(2)}) copy-start(f32[3,256]{1,0:T(4,128)} %param.14) | copy-start | bytes 9220
  7.9 1.5 copy-start.4
  7.9 1.5 copy-start.3
  8.7 0.7 copy-start.2
  8.7 0.7 copy-start
  9.5 0.7 copy-start.7
  11.4 0.7 copy-start.6
  176.1 0.6 copy-start.1
Sparse Core Ops, SparseCore 0:
  101.7 73.6 reduce-scatter.3
where the time goes:
time: 184 us
  blocking collectives  69.5 us (38%)
  waiting for transfers between devices  69.3 us (38%)
  other arithmetic  20.4 us (11%)
  between operations  14.9 us (8%)
  local copies, waits for them, and re-layouts  9.81 us (5%)
    unnamed x2, waiting for transfers between devices  69.3 us
    all_gather x1, blocking collectives, per_device(): group = lax.all_gather(block_data, 'grp', axis=1, tiled=True)  34.8 us
    all_gather x1, blocking collectives, per_device(): targets = lax.all_gather(own_set, 'blk', axis=1, tiled=True)  34.6 us
    reduce_sum x9, other arithmetic, pair_sums(): return jnp.stack([jnp.sum(scaled * term, axis=1) for term in term_list])  18 us
    unnamed x22, local copies, waits for them, and re-layouts  4.44 us
  transfers between devices with their start and end apart: 1, of which 1 were waited for; matrix products, arithmetic and copies ran while one was open for 2% of the time, Pallas kernels for 0%

commit v1 on v0

--- a/solution.py
+++ b/solution.py
@@ -51,7 +51,15 @@
     group = lax.all_gather(block_data, "grp", axis=1, tiled=True)
     group_src = group[:6]
     group_mass = group[6]
-    targets = lax.all_gather(own_set, "blk", axis=1, tiled=True)
+
+    def clear_the_vector(z):
+        base_arr = lax.axis_size("blk")
+        piece_now = jnp.stack([z] * base_arr, 0)
+        local_out = lax.all_to_all(piece_now, axis_name="blk", split_axis=0, concat_axis=0)
+        all_values = jnp.concatenate(local_out, 1)
+        return all_values
+
+    targets = clear_the_vector(own_set)
     blk_size = lax.axis_size("blk")
     blk_here = lax.axis_index("blk")
     block_total = group_src.shape[1] // BLOCK

time: 184 us -> 160 us (0.87)
  blocking collectives: 69.5 us -> 33.9 us
  starting transfers between devices: 0.04 us -> 6.97 us
    all_gather x1 -> x0, blocking collectives: 34.6 us -> none  [per_device(): targets = lax.all_gather(own_set, 'blk', axis=1, tiled=True)]
    all_to_all x0 -> x1, starting transfers between devices: none -> 6.93 us  [clear_the_vector(): lax.all_to_all(piece_now, axis_name='blk', split_axis=0, concat_axis=0)]
    unnamed x22 -> x20, local copies, waits for them, and re-layouts: 4.44 us -> 5.55 us
  transfers between devices with their start and end apart: 1 -> 2, of which waited for: 1 -> 1; matrix products, arithmetic and copies ran while one was open for 2% -> 3% of each run, Pallas kernels for 0% -> 0%
where the time goes in v1:
time: 160 us
  waiting for transfers between devices  70.7 us (44%)
  blocking collectives  33.9 us (21%)
  other arithmetic  21.8 us (14%)
  between operations  14.8 us (9%)
  local copies, waits for them, and re-layouts  11.4 us (7%)
  starting transfers between devices  6.97 us (4%)
    unnamed x2, waiting for transfers between devices  70.6 us
    all_gather x1, blocking collectives, per_device(): group = lax.all_gather(block_data, 'grp', axis=1, tiled=True)  33.9 us
    reduce_sum x9, other arithmetic, pair_sums(): return jnp.stack([jnp.sum(scaled * term, axis=1) for term in term_list])  18 us
    all_to_all x1, starting transfers between devices, clear_the_vector(): lax.all_to_all(piece_now, axis_name='blk', split_axis=0, concat_axis=0)  6.93 us
    unnamed x20, local copies, waits for them, and re-layouts  5.55 us
  transfers between devices with their start and end apart: 2, of which 1 were waited for; matrix products, arithmetic and copies ran while one was open for 3% of the time, Pallas kernels for 0%

profile of v1, /device:TPU:32, one launch (start us, length us, event | category | flops | bytes accessed | tf_op | source)
XLA Modules:
  0.0 160.0 jit_solution(12679471979992692837)
XLA Ops:
  7.2 0.7 broadcast_multiply_fusion
  7.9 0.7 multiply_add_fusion.1
  9.4 0.7 gather_fusion.1
  10.8 0.7 reshape.149
  11.5 6.9 %all-to-all-start = ((f32[8,1,192]{2,1,0:T(1,128)}), f32[8,1,192]{2,1,0:T(1,128)S(1)}, u32[]{:S(2)}, u32[]{:S(2)}) async-start(f32[8,1,192]{2,1,0:T(1,128)} %reshape.149), calls=%async_computation | async-start | bytes 16384 | tf_op jit(solution)/shard_map/all_to_all | solution.py:58
  19.2 0.6 copy-done.6
  19.9 0.7 copy-done.4
  20.6 33.9 %all_gather.3 = f32[7,8192]{1,0:T(8,128)S(1)} all-gather(f32[7,256]{1,0:T(8,128)S(1)} %pad_maximum_fusion), channel_id=1, replica_groups=mesh['blk'=8,'grp'=32] {'grp'}, dimensions={1}, use_global_device_ids=true | all-gather | bytes 236544 | tf_op jit(solution)/shard_map/all_gather | solution.py:51
  55.7 0.7 reduce.12
  56.4 18.5 %while.10 = (s32[]{:T(128)}, f32[8,6,32]{2,1,0:T(8,128)S(1)}, f32[8,64]{1,0:T(8,128)S(1)}, f32[1,8192]{1,0:T(1,128)S(1)}, f32[6,8192]{1,0:T(8,128)S(1)}, /*index=5*/f32[8,6,32]{2,1,0:T(8,128)S(1)}, s32[]{:T(128)}) while((s32[]{:T(128)}, f32[8,6,32]{2,1,0:T(8,128)S(1)}, f32[8,64]{1,0:T(8,128)S(1)}, f32[1,8192]{1,0:T(1,128)S(1)}, ...), condition=%wide.region_8.9_spmd, body=%wide.region_1.8_spmd.sunk | while | flops 10493762 | bytes 703321 | solution.py:80
  56.7 2.0 %fusion.50 = (f32[32]{0:T(128)S(1)}, f32[32]{0:T(128)S(1)}, f32[32]{0:T(128)S(1)}, f32[32]{0:T(128)S(1)}, f32[32]{0:T(128)S(1)}, /*index=5*/f32[32]{0:T(128)S(1)}) fusion(f32[32]{0:T(128)S(1)} %get-tuple-element.171, f32[8192]{0:T(1024)S(1)} %bitcast.113, f32[32]{0:T(128)S(1)} %get-tuple-element.173, f32[8192]{0:T(1024)S(1)} %bitcast.115, ...), kind=kLoop, calls=%fused_computation.25.clone.1 | loop fusion | flops 10485568 | bytes 230912 | tf_op jit(solution)/shard_map/while/body/eval_jaxpr/reduce_sum | solution.py:29
  59.0 2.0 %fusion.50 = (f32[32]{0:T(128)S(1)}, f32[32]{0:T(128)S(1)}, f32[32]{0:T(128)S(1)}, f32[32]{0:T(128)S(1)}, f32[32]{0:T(128)S(1)}, /*index=5*/f32[32]{0:T(128)S(1)}) fusion(f32[32]{0:T(128)S(1)} %get-tuple-element.171, f32[8192]{0:T(1024)S(1)} %bitcast.113, f32[32]{0:T(128)S(1)} %get-tuple-element.173, f32[8192]{0:T(1024)S(1)} %bitcast.115, ...), kind=kLoop, calls=%fused_computation.25.clone.1 | loop fusion | flops 10485568 | bytes 230912 | tf_op jit(solution)/shard_map/while/body/eval_jaxpr/reduce_sum | solution.py:29
  61.3 2.0 %fusion.50 = (f32[32]{0:T(128)S(1)}, f32[32]{0:T(128)S(1)}, f32[32]{0:T(128)S(1)}, f32[32]{0:T(128)S(1)}, f32[32]{0:T(128)S(1)}, /*index=5*/f32[32]{0:T(128)S(1)}) fusion(f32[32]{0:T(128)S(1)} %get-tuple-element.171, f32[8192]{0:T(1024)S(1)} %bitcast.113, f32[32]{0:T(128)S(1)} %get-tuple-element.173, f32[8192]{0:T(1024)S(1)} %bitcast.115, ...), kind=kLoop, calls=%fused_computation.25.clone.1 | loop fusion | flops 10485568 | bytes 230912 | tf_op jit(solution)/shard_map/while/body/eval_jaxpr/reduce_sum | solution.py:29
  63.6 2.0 %fusion.50 = (f32[32]{0:T(128)S(1)}, f32[32]{0:T(128)S(1)}, f32[32]{0:T(128)S(1)}, f32[32]{0:T(128)S(1)}, f32[32]{0:T(128)S(1)}, /*index=5*/f32[32]{0:T(128)S(1)}) fusion(f32[32]{0:T(128)S(1)} %get-tuple-element.171, f32[8192]{0:T(1024)S(1)} %bitcast.113, f32[32]{0:T(128)S(1)} %get-tuple-element.173, f32[8192]{0:T(1024)S(1)} %bitcast.115, ...), kind=kLoop, calls=%fused_computation.25.clone.1 | loop fusion | flops 10485568 | bytes 230912 | tf_op jit(solution)/shard_map/while/body/eval_jaxpr/reduce_sum | solution.py:29
  65.9 2.0 %fusion.50 = (f32[32]{0:T(128)S(1)}, f32[32]{0:T(128)S(1)}, f32[32]{0:T(128)S(1)}, f32[32]{0:T(128)S(1)}, f32[32]{0:T(128)S(1)}, /*index=5*/f32[32]{0:T(128)S(1)}) fusion(f32[32]{0:T(128)S(1)} %get-tuple-element.171, f32[8192]{0:T(1024)S(1)} %bitcast.113, f32[32]{0:T(128)S(1)} %get-tuple-element.173, f32[8192]{0:T(1024)S(1)} %bitcast.115, ...), kind=kLoop, calls=%fused_computation.25.clone.1 | loop fusion | flops 10485568 | bytes 230912 | tf_op jit(solution)/shard_map/while/body/eval_jaxpr/reduce_sum | solution.py:29
  68.3 2.0 %fusion.50 = (f32[32]{0:T(128)S(1)}, f32[32]{0:T(128)S(1)}, f32[32]{0:T(128)S(1)}, f32[32]{0:T(128)S(1)}, f32[32]{0:T(128)S(1)}, /*index=5*/f32[32]{0:T(128)S(1)}) fusion(f32[32]{0:T(128)S(1)} %get-tuple-element.171, f32[8192]{0:T(1024)S(1)} %bitcast.113, f32[32]{0:T(128)S(1)} %get-tuple-element.173, f32[8192]{0:T(1024)S(1)} %bitcast.115, ...), kind=kLoop, calls=%fused_computation.25.clone.1 | loop fusion | flops 10485568 | bytes 230912 | tf_op jit(solution)/shard_map/while/body/eval_jaxpr/reduce_sum | solution.py:29
  70.6 2.0 %fusion.50 = (f32[32]{0:T(128)S(1)}, f32[32]{0:T(128)S(1)}, f32[32]{0:T(128)S(1)}, f32[32]{0:T(128)S(1)}, f32[32]{0:T(128)S(1)}, /*index=5*/f32[32]{0:T(128)S(1)}) fusion(f32[32]{0:T(128)S(1)} %get-tuple-element.171, f32[8192]{0:T(1024)S(1)} %bitcast.113, f32[32]{0:T(128)S(1)} %get-tuple-element.173, f32[8192]{0:T(1024)S(1)} %bitcast.115, ...), kind=kLoop, calls=%fused_computation.25.clone.1 | loop fusion | flops 10485568 | bytes 230912 | tf_op jit(solution)/shard_map/while/body/eval_jaxpr/reduce_sum | solution.py:29
  72.9 2.0 %fusion.50 = (f32[32]{0:T(128)S(1)}, f32[32]{0:T(128)S(1)}, f32[32]{0:T(128)S(1)}, f32[32]{0:T(128)S(1)}, f32[32]{0:T(128)S(1)}, /*index=5*/f32[32]{0:T(128)S(1)}) fusion(f32[32]{0:T(128)S(1)} %get-tuple-element.171, f32[8192]{0:T(1024)S(1)} %bitcast.113, f32[32]{0:T(128)S(1)} %get-tuple-element.173, f32[8192]{0:T(1024)S(1)} %bitcast.115, ...), kind=kLoop, calls=%fused_computation.25.clone.1 | loop fusion | flops 10485568 | bytes 230912 | tf_op jit(solution)/shard_map/while/body/eval_jaxpr/reduce_sum | solution.py:29
  75.0 0.8 copy.100
  75.8 2.0 %fusion.23 = (f32[32]{0:T(128)S(1)}, f32[32]{0:T(128)S(1)}, f32[32]{0:T(128)S(1)}, f32[32]{0:T(128)S(1)}, f32[32]{0:T(128)S(1)}, /*index=5*/f32[32]{0:T(128)S(1)}) fusion(f32[32]{0:T(128)S(1)} %get-tuple-element.74, f32[8192]{0:T(1024)S(1)} %bitcast.122, f32[32]{0:T(128)S(1)} %get-tuple-element.76, f32[8192]{0:T(1024)S(1)} %bitcast.124, ...), kind=kLoop, calls=%fused_computation.69 | loop fusion | flops 10485568 | bytes 230912 | tf_op jit(solution)/shard_map/reduce_sum | solution.py:29
  79.9 0.6 stack.64
  80.5 70.6 %reduce-scatter.4.cloned.1.call-done = f32[32,6]{1,0:T(8,128)} async-done(((f32[256,6]{1,0:T(8,128)}), f32[32,6]{1,0:T(8,128)}) %reduce-scatter.4.cloned.1.call-update) | async-done | bytes 784
  151.2 0.8 copy.99
  152.6 0.6 pad_maximum_fusion.2
  (101 shorter events, 7.7 us)
Async XLA Ops:
  7.2 0.8 copy-start
  8.7 0.7 copy-start.5
  11.5 43.6 %all-to-all-start = ((f32[8,1,192]{2,1,0:T(1,128)}), f32[8,1,192]{2,1,0:T(1,128)S(1)}, u32[]{:S(2)}, u32[]{:S(2)}) async-start(f32[8,1,192]{2,1,0:T(1,128)} %reshape.149), calls=%async_computation | async-start | bytes 16384 | tf_op jit(solution)/shard_map/all_to_all | solution.py:58
  18.4 132.7 %reduce-scatter.4.cloned.1.call-start = ((), (), s32[]{:S(2)}) async-start(), calls=%async_computation.2 | async-start | bytes 147456
  19.1 0.7 copy-start.6
  19.9 0.7 copy-start.4
  75.7 2.0 %copy-start.2 = (f32[3,256]{1,0:T(4,128)S(1)}, f32[3,256]{1,0:T(4,128)}, u32[]{:S(2)}) copy-start(f32[3,256]{1,0:T(4,128)} %param.15) | copy-start | bytes 9220
  77.8 0.7 copy-start.3
  151.9 0.6 copy-start.1
Sparse Core Ops, SparseCore 0:
  75.9 75.2 reduce-scatter.3
